TPU v7x, 256 devices: a whole 4x4x8 slice. The times are simulated.
256 devices in a mesh: seq: 64 (over y, z, core), ch: 4 (over x).
Axes of the slice: x: 4, y: 4, z: 8, core: 2. Of those that a mesh axis runs over, the one named last changes fastest.
Arguments:
- query_stream: bfloat16 [16384, 4096], P('seq', 'ch'), may hold values from -16 to 16
- key_stream: bfloat16 [16384, 4096], P('seq', 'ch'), may hold values from -6 to 6
- value_stream: bfloat16 [16384, 4096], P('seq', 'ch'), may hold values from -6 to 6
- filter_taps: float32 [4096, 128], P('ch'), may hold values from -0.5 to 0.5
- out_weight: bfloat16 [4096, 4096], P('seq', 'ch'), may hold values from -0.09375 to 0.09375
- upstream: bfloat16 [16384, 4096], P('seq', 'ch'), may hold values from -6 to 6
Outputs:
- mixed: bfloat16 [16384, 4096], P('seq', 'ch')
- grad_query: bfloat16 [16384, 4096], P('seq', 'ch')
- grad_key: bfloat16 [16384, 4096], P('seq', 'ch')
- grad_value: bfloat16 [16384, 4096], P('seq', 'ch')
- grad_filter: float32 [4096, 128], P('ch')
- grad_weight: float32 [4096, 4096], P('seq', 'ch')
All inputs are finite; a program needn't handle non-finite values.
Results may differ from a plain program's by a relative error of at most 0.0057.
Values may be sent and summed in bfloat16 or wider, within the bound.
No kernel may reach another device: no remote copies, remote signals or barrier semaphores. Data moves between devices by JAX's collectives and lax.ppermute only.
A program may use at most 128 MiB of HBM per device.

v0:
```python
import jax
import jax.numpy as jnp
from jax import lax
from jax.sharding import PartitionSpec as P


def from_behind(value, axis, steps):
    count = lax.axis_size(axis)
    initial, last = (max(0, -steps), min(count, count - steps))
    return lax.ppermute(value, axis, [(source, source + steps) for source in range(initial, last)])


def depthwise(signal, kernel):
    output = lax.conv_general_dilated(
        signal[None],
        kernel[:, None, :],
        (1,),
        "VALID",
        dimension_numbers=("NWC", "WIO", "NWC"),
        feature_group_count=signal.shape[1],
        precision=lax.Precision.HIGHEST,
    )
    return output[0]


def body(query_stream, key_stream, value_stream, filter_taps, out_weight, upstream):
    rows_here = query_stream.shape[0]
    tap_count = filter_taps.shape[1]
    keyed = (key_stream.astype(jnp.float32) * value_stream.astype(jnp.float32)).astype(jnp.bfloat16)
    rim_before = from_behind(keyed[rows_here - (tap_count - 1) :], "seq", 1)
    front_pad = jnp.concatenate([rim_before, keyed], axis=0).astype(jnp.float32)
    response = depthwise(front_pad, filter_taps.T[::-1])
    query_wide = query_stream.astype(jnp.float32)
    gated = (query_wide * response).astype(jnp.bfloat16)
    gated_full = lax.all_gather(gated, "ch", axis=1, tiled=True)
    weight_cols = lax.all_gather(out_weight, "seq", axis=0, tiled=True)
    mixed = jnp.dot(gated_full, weight_cols, preferred_element_type=jnp.float32).astype(
        jnp.bfloat16
    )
    partial_terms = lax.dot_general(
        upstream, weight_cols, (((1,), (1,)), ((), ())), preferred_element_type=jnp.float32
    )
    grad_gated = lax.psum_scatter(partial_terms, "ch", scatter_dimension=1, tiled=True)
    grad_query = (grad_gated * response).astype(jnp.bfloat16)
    grad_response = grad_gated * query_wide
    rim_after = from_behind(grad_response[: tap_count - 1], "seq", -1)
    back_pad = jnp.concatenate([grad_response, rim_after], axis=0)
    grad_keyed = depthwise(back_pad, filter_taps.T)
    grad_key = (grad_keyed * value_stream.astype(jnp.float32)).astype(jnp.bfloat16)
    grad_value = (grad_keyed * key_stream.astype(jnp.float32)).astype(jnp.bfloat16)
    filter_local = depthwise(front_pad, grad_response)[::-1].T
    grad_filter = lax.psum(filter_local, "seq")
    columns = lax.slice_in_dim(gated_full, 0, lax.axis_size("seq") * out_weight.shape[0], axis=1)
    grad_weight = lax.psum_scatter(
        lax.dot_general(
            columns, upstream, (((0,), (0,)), ((), ())), preferred_element_type=jnp.float32
        ),
        "seq",
        scatter_dimension=0,
        tiled=True,
    )
    return (mixed, grad_query, grad_key, grad_value, grad_filter, grad_weight)


def solution(mesh):
    in_specs = (
        P("seq", "ch"),
        P("seq", "ch"),
        P("seq", "ch"),
        P("ch", None),
        P("seq", "ch"),
        P("seq", "ch"),
    )
    out_specs = (
        P("seq", "ch"),
        P("seq", "ch"),
        P("seq", "ch"),
        P("seq", "ch"),
        P("ch", None),
        P("seq", "ch"),
    )
    return jax.shard_map(body, mesh=mesh, in_specs=in_specs, out_specs=out_specs, check_vma=False)
```

profile of v0, /device:TPU:2, one launch (start us, length us, event | category | flops | bytes accessed | tf_op | source)
XLA Modules:
  0.0 614.4 jit_solution(9339220841736007042)
XLA Ops:
  7.2 0.7 all-gather.5.cloned.1.call-update
  8.0 88.8 %all-gather.5.cloned.1.call-done = bf16[4096,1024]{1,0:T(8,128)(2,1)} async-done(((bf16[64,1024]{1,0:T(8,128)(2,1)}), bf16[4096,1024]{1,0:T(8,128)(2,1)}) %all-gather.5.cloned.1.call-update) | async-done | bytes 8388624 | tf_op jit(solution)/shard_map/all_gather | solution.py:36
  96.8 7.7 %fusion.12 = f32[256,4096]{1,0:T(8,128)} fusion(bf16[256,1024]{1,0:T(8,128)(2,1)S(1)} %copy-done, bf16[4096,1024]{1,0:T(8,128)(2,1)} %all-gather.5.cloned.1.call-done), kind=kOutput, calls=%fused_computation.22 | convolution fusion | flops 2147483648 | bytes 13107200 | tf_op jit(solution)/shard_map/dot_general | solution.py:40
  104.5 45.0 %reduce-scatter.3.cloned.1.call-done = f32[256,1024]{1,0:T(8,128)} async-done(((f32[256,4096]{1,0:T(8,128)}), f32[256,1024]{1,0:T(8,128)}) %reduce-scatter.3.cloned.1.call-update) | async-done | bytes 1048592 | tf_op jit(solution)/shard_map/reduce_scatter | solution.py:43
  149.5 1.4 convert_multiply_fusion.3
  151.0 1.3 collective-permute-start.1
  152.3 0.4 copy.20
  152.7 2.2 collective-permute-done.1
  154.9 1.2 maximum_bitcast_fusion
  156.1 10.6 %fusion = f32[1,256,1024]{2,0,1:T(1,128)S(1)} fusion(f32[128,1,1024]{2,1,0:T(1,128)S(1)} %copy.20, f32[1,383,1024]{2,1,0:T(8,128)S(1)} %maximum_bitcast_fusion), kind=kOutput, calls=%fused_computation.1 | convolution fusion | flops 402653184 | bytes 3141632 | tf_op jit(solution)/shard_map/conv_general_dilated | solution.py:14
  166.7 1.5 fusion.7
  168.3 8.5 %collective-permute-start = (bf16[127,1024]{1,0:T(8,128)(2,1)S(1)}, bf16[127,1024]{1,0:T(8,128)(2,1)S(1)}, u32[]{:S(2)}, u32[]{:S(2)}) collective-permute-start(bf16[127,1024]{1,0:T(8,128)(2,1)S(1)} %slice.8), channel_id=1, source_target_pairs={{0,4},{4,8},{8,12},{12,16},{16,20},{20,24},{24,28},{28,32},{32,36}... | collective-permute-start | bytes 780296 | tf_op jit(solution)/shard_map/ppermute | solution.py:10
  176.8 0.7 rev.6
  177.6 0.4 copy.18
  178.2 10.6 %fusion.4 = f32[1,256,1024]{2,0,1:T(1,128)S(1)} fusion(f32[128,1,1024]{2,1,0:T(1,128)S(1)} %copy.18, bf16[1,383,1024]{2,1,0:T(8,128)(2,1)S(1)} %maximum_bitcast_fusion.1), kind=kOutput, calls=%fused_computation.11 | convolution fusion | flops 402653184 | bytes 2357248 | tf_op jit(solution)/shard_map/conv_general_dilated | solution.py:14
  188.8 1.4 fusion.10
  190.3 10.7 %fusion.2 = f32[1,128,1024]{2,0,1:T(1,128)S(1)} fusion(bf16[1,383,1024]{2,1,0:T(8,128)(2,1)S(1)} %maximum_bitcast_fusion.1, f32[256,1,1024]{2,0,1:T(8,128)S(1)} %bitcast.29), kind=kOutput, calls=%fused_computation.9 | convolution fusion | flops 402653184 | bytes 2357248 | tf_op jit(solution)/shard_map/conv_general_dilated | solution.py:14
  201.1 2.6 rev.7
  203.9 23.9 %all-gather.3.cloned.1.call-done = bf16[256,4096]{1,0:T(8,128)(2,1)} async-done(((bf16[256,1024]{1,0:T(8,128)(2,1)}), bf16[256,4096]{1,0:T(8,128)(2,1)}) %all-gather.3.cloned.1.call-update) | async-done | bytes 2097168 | tf_op jit(solution)/shard_map/all_gather | solution.py:35
  227.9 9.7 %fusion.13 = f32[4096,1024]{1,0:T(8,128)} fusion(bf16[256,4096]{1,0:T(8,128)(2,1)} %all-gather.3.cloned.1.call-done, bf16[256,1024]{1,0:T(8,128)(2,1)S(1)} %copy-done), kind=kOutput, calls=%fused_computation.23 | convolution fusion | flops 2147483648 | bytes 19398656 | tf_op jit(solution)/shard_map/dot_general | solution.py:55
  237.6 178.5 %all-reduce.2.cloned.1.call-done = f32[1024,128]{0,1:T(8,128)} async-done(((f32[1024,128]{0,1:T(8,128)}), f32[1024,128]{0,1:T(8,128)}) %all-reduce.2.cloned.1.call-update) | async-done | bytes 524304 | tf_op jit(solution)/shard_map/psum | solution.py:52
  416.1 2.0 copy.23
  418.1 6.5 %convolution_convert_fusion = bf16[256,1024]{1,0:T(8,128)(2,1)} fusion(bf16[256,4096]{1,0:T(8,128)(2,1)S(1)} %copy-done.4, bf16[4096,1024]{1,0:T(8,128)(2,1)} %all-gather.5.cloned.1.call-done), kind=kOutput, calls=%fused_computation.8 | convolution fusion | flops 2147745792 | bytes 11010048 | tf_op jit(solution)/shard_map/dot_general | solution.py:37
  424.6 183.2 %reduce-scatter.5.cloned.1.call-done = f32[64,1024]{1,0:T(8,128)} async-done(((f32[4096,1024]{1,0:T(8,128)}), f32[64,1024]{1,0:T(8,128)}) %reduce-scatter.5.cloned.1.call-update) | async-done | bytes 262160 | tf_op jit(solution)/shard_map/reduce_scatter | solution.py:54
  (36 shorter events, 0.8 us)
Async XLA Ops:
  7.2 89.6 %copy-start = (bf16[256,1024]{1,0:T(8,128)(2,1)S(1)}, bf16[256,1024]{1,0:T(8,128)(2,1)}, u32[]{:S(2)}) copy-start(bf16[256,1024]{1,0:T(8,128)(2,1)} %param.11) | copy-start | bytes 1572868
  7.2 89.6 %all-gather.5.cloned.1.call-start = ((), (), s32[]{:S(2)}) async-start(), calls=%async_computation.3 | async-start | bytes 8519680 | tf_op jit(solution)/shard_map/all_gather | solution.py:36
  7.9 141.6 %reduce-scatter.3.cloned.1.call-start = ((), (), s32[]{:S(2)}) async-start(), calls=%async_computation.4 | async-start | bytes 5242880 | tf_op jit(solution)/shard_map/reduce_scatter | solution.py:43
  104.4 45.1 %copy-start.5 = (bf16[256,1024]{1,0:T(8,128)(2,1)S(1)}, bf16[256,1024]{1,0:T(8,128)(2,1)}, u32[]{:S(2)}) copy-start(bf16[256,1024]{1,0:T(8,128)(2,1)} %param.6) | copy-start | bytes 1572868
  104.5 47.8 %copy-start.7 = (f32[1024,128]{1,0:T(8,128)S(1)}, f32[1024,128]{1,0:T(8,128)}, u32[]{:S(2)}) copy-start(f32[1024,128]{1,0:T(8,128)} %param.9) | copy-start | bytes 1572868
  104.5 123.4 %all-gather.3.cloned.1.call-start = ((), (), s32[]{:S(2)}) async-start(), calls=%async_computation.2 | async-start | bytes 2621440 | tf_op jit(solution)/shard_map/all_gather | solution.py:35
  150.9 5.2 copy-start.1
  151.0 3.9 collective-permute-start.1
  156.1 10.6 %copy-start.9 = (bf16[256,1024]{1,0:T(8,128)(2,1)S(1)}, bf16[256,1024]{1,0:T(8,128)(2,1)}, u32[]{:S(2)}) copy-start(bf16[256,1024]{1,0:T(8,128)(2,1)} %param.7) | copy-start | bytes 1572868
  156.1 10.6 %copy-start.10 = (bf16[256,1024]{1,0:T(8,128)(2,1)S(1)}, bf16[256,1024]{1,0:T(8,128)(2,1)}, u32[]{:S(2)}) copy-start(bf16[256,1024]{1,0:T(8,128)(2,1)} %param.8) | copy-start | bytes 1572868
  166.7 10.1 %copy-start.8 = (f32[1024,128]{1,0:T(8,128)S(1)}, f32[1024,128]{1,0:T(8,128)}, u32[]{:S(2)}) copy-start(f32[1024,128]{1,0:T(8,128)} %param.9) | copy-start | bytes 1572868
  168.3 9.7 %collective-permute-start = (bf16[127,1024]{1,0:T(8,128)(2,1)S(1)}, bf16[127,1024]{1,0:T(8,128)(2,1)S(1)}, u32[]{:S(2)}, u32[]{:S(2)}) collective-permute-start(bf16[127,1024]{1,0:T(8,128)(2,1)S(1)} %slice.8), channel_id=1, source_target_pairs={{0,4},{4,8},{8,12},{12,16},{16,20},{20,24},{24,28},{28,32},{32,36}... | collective-permute-start | bytes 780296 | tf_op jit(solution)/shard_map/ppermute | solution.py:10
  178.1 10.6 %copy-start.3 = (f32[256,1024]{1,0:T(8,128)S(1)}, f32[256,1024]{1,0:T(8,128)}, u32[]{:S(2)}) copy-start(f32[256,1024]{1,0:T(8,128)} %reduce-scatter.3.cloned.1.call-done) | copy-start | bytes 3145732
  178.1 10.6 %copy-start.6 = (bf16[256,1024]{1,0:T(8,128)(2,1)S(1)}, bf16[256,1024]{1,0:T(8,128)(2,1)}, u32[]{:S(2)}) copy-start(bf16[256,1024]{1,0:T(8,128)(2,1)} %param.6) | copy-start | bytes 1572868
  188.8 1.5 copy-start.2
  190.2 225.9 %all-reduce.2.cloned.1.call-start = ((), (), s32[]{:S(2)}) async-start(), calls=%async_computation.5 | async-start | bytes 1048576 | tf_op jit(solution)/shard_map/psum | solution.py:52
  203.7 404.1 %reduce-scatter.5.cloned.1.call-start = ((), (), s32[]{:S(2)}) async-start(), calls=%async_computation.6 | async-start | bytes 17039360 | tf_op jit(solution)/shard_map/reduce_scatter | solution.py:54
  237.6 180.5 %copy-start.4 = (bf16[256,4096]{1,0:T(8,128)(2,1)S(1)}, bf16[256,4096]{1,0:T(8,128)(2,1)}, u32[]{:S(2)}) copy-start(bf16[256,4096]{1,0:T(8,128)(2,1)} %all-gather.3.cloned.1.call-done) | copy-start | bytes 6291460
Sparse Core Ops, SparseCore 0:
  10.8 85.9 all-gather.4
  104.6 44.8 reduce-scatter.2
  190.4 37.4 all-gather.2
  231.8 184.2 all-reduce.1
  421.0 186.7 reduce-scatter.4
where the time goes:
time: 615 us; the launch traced here: 614 us
  waiting for transfers between devices  522 us (85%)
  matrix products  55.7 us (9%)
  between operations  14 us (2%)
  starting transfers between devices  10.2 us (2%)
  local copies, waits for them, and re-layouts  6.47 us (1%)
    reduce_scatter x1, waiting for transfers between devices, body(): lax.psum_scatter(lax.dot_general(columns, upstream, (((0,), (0,)), ((), (...  183 us
    psum x1, waiting for transfers between devices, body(): grad_filter = lax.psum(filter_local, 'seq')  178 us
    all_gather x1, waiting for transfers between devices, body(): weight_cols = lax.all_gather(out_weight, 'seq', axis=0, tiled=True)  88.8 us
    reduce_scatter x1, waiting for transfers between devices, body(): lax.psum_scatter(partial_terms, 'ch', scatter_dimension=1, tiled=True)  45 us
    conv_general_dilated x3, matrix products, depthwise(): lax.conv_general_dilated(signal[None], kernel[:, None, :], (1,), 'VALID',...  31.8 us
    all_gather x1, waiting for transfers between devices, body(): gated_full = lax.all_gather(gated, 'ch', axis=1, tiled=True)  23.9 us
  transfers between devices with their start and end apart: 7, of which 6 were waited for; matrix products, arithmetic and copies ran while one was open for 5% of the time, Pallas kernels for 0%

commit v1 on v0

v1 whole, which is shorter than its diff:
```python
import jax
import jax.numpy as jnp
from jax import lax
from jax.sharding import Mesh
from jax.sharding import PartitionSpec as P

SUB = ("sy", "sz", "sc")


def seq_factors(mesh):
    count = mesh.shape["seq"]
    try:
        devices = list(mesh.devices[:, 0])
        cores = len({d.core_on_chip for d in devices})
        zs = len({d.coords[2] for d in devices})
        if cores * zs and count % (cores * zs) == 0:
            return (count // (cores * zs), zs, cores)
    except Exception:
        pass
    return (count // 16, 8, 2) if count % 16 == 0 else (1, 1, count)


def from_behind(value, axis, count, steps):
    initial, last = (max(0, -steps), min(count, count - steps))
    return lax.ppermute(value, axis, [(source, source + steps) for source in range(initial, last)])


def depthwise(signal, kernel):
    output = lax.conv_general_dilated(
        signal[None],
        kernel[:, None, :],
        (1,),
        "VALID",
        dimension_numbers=("NWC", "WIO", "NWC"),
        feature_group_count=signal.shape[1],
        precision=lax.Precision.HIGHEST,
    )
    return output[0]


def gather_ch(part, count):
    here = lax.axis_index("ch")
    pieces = [part] + [
        lax.ppermute(part, "ch", [(i, (i + k) % count) for i in range(count)]) for k in range(1, count)
    ]
    stacked = jnp.stack(pieces)[(here - jnp.arange(count)) % count]
    return jnp.concatenate([stacked[j] for j in range(count)], axis=1)


def scatter_ch(whole, count):
    here = lax.axis_index("ch")
    width = whole.shape[1] // count
    total = lax.dynamic_slice_in_dim(whole, here * width, width, 1)
    for k in range(1, count):
        block = lax.dynamic_slice_in_dim(whole, ((here + k) % count) * width, width, 1)
        total = total + lax.ppermute(block, "ch", [(i, (i + k) % count) for i in range(count)])
    return total


def butterfly_sum(value, factors):
    for axis, size in zip(SUB, factors):
        bit = 1
        while bit < size:
            value = value + lax.ppermute(value, axis, [(i, i ^ bit) for i in range(size)])
            bit *= 2
    return value


def make_body(factors, chs):
    n_seq = factors[0] * factors[1] * factors[2]

    def body(query_stream, key_stream, value_stream, filter_taps, out_weight, upstream):
        rows_here = query_stream.shape[0]
        tap_count = filter_taps.shape[1]
        keyed = (key_stream.astype(jnp.float32) * value_stream.astype(jnp.float32)).astype(jnp.bfloat16)
        rim_before = from_behind(keyed[rows_here - (tap_count - 1) :], SUB, n_seq, 1)
        front_pad = jnp.concatenate([rim_before, keyed], axis=0).astype(jnp.float32)
        response = depthwise(front_pad, filter_taps.T[::-1])
        query_wide = query_stream.astype(jnp.float32)
        gated = (query_wide * response).astype(jnp.bfloat16)
        gated_full = gather_ch(gated, chs)
        weight_cols = lax.all_gather(out_weight, SUB, axis=0, tiled=True)
        mixed = jnp.dot(gated_full, weight_cols, preferred_element_type=jnp.float32).astype(
            jnp.bfloat16
        )
        partial_terms = lax.dot_general(
            upstream, weight_cols, (((1,), (1,)), ((), ())), preferred_element_type=jnp.float32
        )
        grad_gated = scatter_ch(partial_terms, chs)
        grad_query = (grad_gated * response).astype(jnp.bfloat16)
        grad_response = grad_gated * query_wide
        rim_after = from_behind(grad_response[: tap_count - 1], SUB, n_seq, -1)
        back_pad = jnp.concatenate([grad_response, rim_after], axis=0)
        grad_keyed = depthwise(back_pad, filter_taps.T)
        grad_key = (grad_keyed * value_stream.astype(jnp.float32)).astype(jnp.bfloat16)
        grad_value = (grad_keyed * key_stream.astype(jnp.float32)).astype(jnp.bfloat16)
        filter_local = depthwise(front_pad, grad_response)[::-1].T
        grad_filter = butterfly_sum(filter_local, factors)
        block = out_weight.shape[0]
        columns = lax.slice_in_dim(gated_full, 0, n_seq * block, axis=1)
        columns = columns.reshape((rows_here,) + factors + (block,)).transpose(0, 3, 2, 1, 4)
        columns = columns.reshape(rows_here, n_seq * block)
        partial = lax.dot_general(
            columns, upstream, (((0,), (0,)), ((), ())), preferred_element_type=jnp.float32
        )
        for axis in ("sc", "sz", "sy"):
            partial = lax.psum_scatter(partial, axis, scatter_dimension=0, tiled=True)
        return (mixed, grad_query, grad_key, grad_value, grad_filter, partial)

    return body


def solution(mesh):
    factors = seq_factors(mesh)
    chs = mesh.shape["ch"]
    fine = Mesh(mesh.devices.reshape(factors + (chs,)), SUB + ("ch",))
    rows = P(SUB, "ch")
    in_specs = (rows, rows, rows, P("ch", None), rows, rows)
    out_specs = (rows, rows, rows, rows, P("ch", None), rows)
    return jax.shard_map(
        make_body(factors, chs), mesh=fine, in_specs=in_specs, out_specs=out_specs, check_vma=False
    )
```

time: 615 us -> 452 us (0.73)
  waiting for transfers between devices: 522 us -> 327 us
  starting transfers between devices: 10.2 us -> 32.2 us
  local copies, waits for them, and re-layouts: 6.47 us -> 14.8 us
    psum x1 -> x0, waiting for transfers between devices: 178 us -> none  [body(): grad_filter = lax.psum(filter_local, 'seq')]
    ppermute x0 -> x12, waiting for transfers between devices: none -> 140 us  [the longest x6 71.4 us: butterfly_sum(): lax.ppermute(value, axis, [(i, i ^ bit) for i in range(size)])]
    reduce_scatter x2 -> x3, waiting for transfers between devices: 228 us -> 95 us  [body(): partial = lax.psum_scatter(partial, axis, scatter_dimension=0, tiled=True)]
    all_gather x2 -> x1, waiting for transfers between devices: 113 us -> 88.7 us  [body(): weight_cols = lax.all_gather(out_weight, SUB, axis=0, tiled=True)]
    ppermute x0 -> x12, starting transfers between devices: none -> 22.6 us  [the longest x6 14.1 us: butterfly_sum(): lax.ppermute(value, axis, [(i, i ^ bit) for i in range(size)])]
  transfers between devices with their start and end apart: 7 -> 18, of which waited for: 6 -> 14; matrix products, arithmetic and copies ran while one was open for 5% -> 5% of each run, Pallas kernels for 0% -> 0%
where the time goes in v1:
time: 452 us; the launch traced here: 450 us
  waiting for transfers between devices  327 us (72%)
  matrix products  52.3 us (12%)
  starting transfers between devices  32.2 us (7%)
  local copies, waits for them, and re-layouts  14.8 us (3%)
  between operations  14.3 us (3%)
  other arithmetic  10 us (2%)
    reduce_scatter x3, waiting for transfers between devices, body(): partial = lax.psum_scatter(partial, axis, scatter_dimension=0, tiled=True)  95 us
    all_gather x1, waiting for transfers between devices, body(): weight_cols = lax.all_gather(out_weight, SUB, axis=0, tiled=True)  88.7 us
    ppermute x6, waiting for transfers between devices, butterfly_sum(): lax.ppermute(value, axis, [(i, i ^ bit) for i in range(size)])  71.4 us
    ppermute x3, waiting for transfers between devices, scatter_ch(): lax.ppermute(block, 'ch', [(i, (i + k) % count) for i in range(count)])  45.8 us
    conv_general_dilated x3, matrix products, depthwise(): lax.conv_general_dilated(signal[None], kernel[:, None, :], (1,), 'VALID',...  31.8 us
    ppermute x3, waiting for transfers between devices, gather_ch(): lax.ppermute(part, 'ch', [(i, (i + k) % count) for i in range(count)])  22.8 us
    ppermute x6, starting transfers between devices, butterfly_sum(): lax.ppermute(value, axis, [(i, i ^ bit) for i in range(size)])  14.1 us
    ppermute x2, starting transfers between devices, from_behind(): lax.ppermute(value, axis, [(source, source + steps) for source in range(i...  9.47 us
  transfers between devices with their start and end apart: 18, of which 14 were waited for; matrix products, arithmetic and copies ran while one was open for 5% of the time, Pallas kernels for 0%

profile of v1, /device:TPU:2, one launch (start us, length us, event | category | flops | bytes accessed | tf_op | source)
XLA Modules:
  0.0 450.2 jit_solution(6935114478768854161)
XLA Ops:
  8.0 88.7 %all-gather.2.cloned.1.call-done = bf16[4096,1024]{1,0:T(8,128)(2,1)} async-done(((bf16[64,1024]{1,0:T(8,128)(2,1)}), bf16[4096,1024]{1,0:T(8,128)(2,1)}) %all-gather.2.cloned.1.call-update) | async-done | bytes 8388624 | tf_op jit(solution)/shard_map/all_gather | solution.py:82
  96.8 5.7 %fusion.27 = f32[256,4096]{1,0:T(8,128)S(1)} fusion(bf16[256,1024]{1,0:T(8,128)(2,1)S(1)} %copy-done, bf16[4096,1024]{1,0:T(8,128)(2,1)} %all-gather.2.cloned.1.call-done), kind=kOutput, calls=%fused_computation.51 | convolution fusion | flops 2147483648 | bytes 13107200 | tf_op jit(solution)/shard_map/dot_general | solution.py:86
  109.5 22.1 %collective-permute-done.4 = f32[256,1024]{1,0:T(8,128)S(1)} collective-permute-done((f32[256,1024]{1,0:T(8,128)}, f32[256,1024]{1,0:T(8,128)S(1)}, u32[]{:S(2)}, u32[]{:S(2)}) %collective-permute-start.4) | collective-permute-done | bytes 1048608 | tf_op jit(solution)/shard_map/ppermute | solution.py:56
  132.6 22.7 %collective-permute-done.5 = f32[256,1024]{1,0:T(8,128)} collective-permute-done((f32[256,1024]{1,0:T(8,128)}, f32[256,1024]{1,0:T(8,128)}, u32[]{:S(2)}, u32[]{:S(2)}) %collective-permute-start.5) | collective-permute-done | bytes 1048608 | tf_op jit(solution)/shard_map/ppermute | solution.py:56
  155.3 3.7 convert_multiply_fusion.3
  164.3 10.6 %fusion.8 = f32[1,256,1024]{2,0,1:T(1,128)S(1)} fusion(f32[128,1,1024]{2,1,0:T(1,128)S(1)} %copy.20, f32[1,383,1024]{2,1,0:T(8,128)S(1)} %maximum_bitcast_fusion.1), kind=kOutput, calls=%fused_computation.12 | convolution fusion | flops 402653184 | bytes 3141632 | tf_op jit(solution)/shard_map/conv_general_dilated | solution.py:29
  176.4 8.2 %collective-permute-start = (bf16[127,1024]{1,0:T(8,128)(2,1)S(1)}, bf16[127,1024]{1,0:T(8,128)(2,1)S(1)}, u32[]{:S(2)}, u32[]{:S(2)}) collective-permute-start(bf16[127,1024]{1,0:T(8,128)(2,1)S(1)} %slice.26), channel_id=1, source_target_pairs={{0,4},{4,8},{8,12},{12,16},{16,20},{20,24},{24,28},{28,32},{32,36}... | collective-permute-start | bytes 780296 | tf_op jit(solution)/shard_map/ppermute | solution.py:25
  186.0 10.6 %fusion.15 = f32[1,256,1024]{2,0,1:T(1,128)S(1)} fusion(f32[128,1,1024]{2,1,0:T(1,128)S(1)} %copy.18, bf16[1,383,1024]{2,1,0:T(8,128)(2,1)S(1)} %maximum_bitcast_fusion.2), kind=kOutput, calls=%fused_computation.22 | convolution fusion | flops 402653184 | bytes 2357248 | tf_op jit(solution)/shard_map/conv_general_dilated | solution.py:29
  199.6 2.6 collective-permute-start.1
  202.3 9.7 %collective-permute-done.3 = bf16[256,1024]{1,0:T(8,128)(2,1)S(1)} collective-permute-done((bf16[256,1024]{1,0:T(8,128)(2,1)S(1)}, bf16[256,1024]{1,0:T(8,128)(2,1)S(1)}, u32[]{:S(2)}, u32[]{:S(2)}) %collective-permute-start.3) | collective-permute-done | bytes 524320 | tf_op jit(solution)/shard_map/ppermute | solution.py:44
  212.0 10.3 %collective-permute-done.2 = bf16[256,1024]{1,0:T(8,128)(2,1)S(1)} collective-permute-done((bf16[256,1024]{1,0:T(8,128)(2,1)S(1)}, bf16[256,1024]{1,0:T(8,128)(2,1)S(1)}, u32[]{:S(2)}, u32[]{:S(2)}) %collective-permute-start.2) | collective-permute-done | bytes 524320 | tf_op jit(solution)/shard_map/ppermute | solution.py:44
  222.3 2.8 collective-permute-done.1
  234.5 8.1 %fusion.28 = f32[4096,1024]{1,0:T(8,128)} fusion(bf16[256,4096]{0,1:T(8,128)(2,1)S(1)} %bitcast.50, bf16[256,1024]{1,0:T(8,128)(2,1)S(1)} %copy-done), kind=kOutput, calls=%fused_computation.52 | convolution fusion | flops 2147483648 | bytes 19398656 | tf_op jit(solution)/shard_map/dot_general | solution.py:103
  242.7 29.8 %reduce-scatter.4.cloned.1.call-done = f32[2048,1024]{1,0:T(8,128)} async-done(((f32[4096,1024]{1,0:T(8,128)}), f32[2048,1024]{1,0:T(8,128)}) %reduce-scatter.4.cloned.1.call-update) | async-done | bytes 8388624 | tf_op jit(solution)/shard_map/reduce_scatter | solution.py:107
  273.9 10.6 %fusion.13 = f32[1,128,1024]{2,0,1:T(1,128)S(1)} fusion(bf16[1,383,1024]{2,1,0:T(8,128)(2,1)S(1)} %copy-done.12, f32[256,1,1024]{2,0,1:T(8,128)S(1)} %bitcast.51), kind=kOutput, calls=%fused_computation.20 | convolution fusion | flops 402653184 | bytes 2357248 | tf_op jit(solution)/shard_map/conv_general_dilated | solution.py:29
  286.5 12.5 %collective-permute-done.8 = f32[1024,128]{0,1:T(8,128)S(1)} collective-permute-done((f32[1024,128]{0,1:T(8,128)S(1)}, f32[1024,128]{0,1:T(8,128)S(1)}, u32[]{:S(2)}, u32[]{:S(2)}) %collective-permute-start.8) | collective-permute-done | bytes 524320 | tf_op jit(solution)/shard_map/ppermute | solution.py:64
  299.1 3.1 collective-permute-start.9
  302.2 11.7 %collective-permute-done.9 = f32[1024,128]{0,1:T(8,128)S(1)} collective-permute-done((f32[1024,128]{0,1:T(8,128)S(1)}, f32[1024,128]{0,1:T(8,128)S(1)}, u32[]{:S(2)}, u32[]{:S(2)}) %collective-permute-start.9) | collective-permute-done | bytes 524320 | tf_op jit(solution)/shard_map/ppermute | solution.py:64
  315.6 65.2 %reduce-scatter.6.cloned.1.call-done = f32[256,1024]{1,0:T(8,128)} async-done(((f32[2048,1024]{1,0:T(8,128)}), f32[256,1024]{1,0:T(8,128)}) %reduce-scatter.6.cloned.1.call-update) | async-done | bytes 1048592 | tf_op jit(solution)/shard_map/reduce_scatter | solution.py:107
  380.9 2.6 collective-permute-start.11
  383.6 23.1 %collective-permute-done.11 = f32[1024,128]{0,1:T(8,128)S(1)} collective-permute-done((f32[1024,128]{0,1:T(8,128)S(1)}, f32[1024,128]{0,1:T(8,128)S(1)}, u32[]{:S(2)}, u32[]{:S(2)}) %collective-permute-start.11) | collective-permute-done | bytes 524320 | tf_op jit(solution)/shard_map/ppermute | solution.py:64
  406.8 5.0 %collective-permute-start.12 = (f32[1024,128]{0,1:T(8,128)S(1)}, f32[1024,128]{0,1:T(8,128)S(1)}, u32[]{:S(2)}, u32[]{:S(2)}) collective-permute-start(f32[1024,128]{0,1:T(8,128)S(1)} %add.105), channel_id=1, source_target_pairs={{0,32},{8,40},{16,48},{24,56},{32,0},{40,8},{48,16},{56,24},{1,33}... | collective-permute-start | bytes 1572872 | tf_op jit(solution)/shard_map/ppermute | solution.py:64
  411.8 24.1 %collective-permute-done.12 = f32[1024,128]{0,1:T(8,128)S(1)} collective-permute-done((f32[1024,128]{0,1:T(8,128)S(1)}, f32[1024,128]{0,1:T(8,128)S(1)}, u32[]{:S(2)}, u32[]{:S(2)}) %collective-permute-start.12) | collective-permute-done | bytes 524320 | tf_op jit(solution)/shard_map/ppermute | solution.py:64
  436.0 6.6 %fusion.10 = bf16[256,1024]{1,0:T(8,128)(2,1)} fusion(bf16[4096,1024]{1,0:T(8,128)(2,1)} %all-gather.2.cloned.1.call-done, bf16[256,1024]{1,0:T(8,128)(2,1)S(1)} %copy-done.18, bf16[256,1024]{1,0:T(8,128)(2,1)S(1)} %copy-done.17, bf16[256,1024]{1,0:T(8,128)(2,1)S(1)} %copy-done.16, bf16[256,1024]{1,0:T(8,128)(2,1)S(1)} %copy-done.15), kind=kOutput, calls=%fused_computation.19 | convolution fusion | flops 2156134400 | bytes 11010048 | tf_op jit(solution)/shard_map/dot_general | solution.py:83
  (91 shorter events, 35.6 us)
Async XLA Ops:
  7.2 89.6 %copy-start = (bf16[256,1024]{1,0:T(8,128)(2,1)S(1)}, bf16[256,1024]{1,0:T(8,128)(2,1)}, u32[]{:S(2)}) copy-start(bf16[256,1024]{1,0:T(8,128)(2,1)} %param.11) | copy-start | bytes 1572868
  7.2 89.6 %all-gather.2.cloned.1.call-start = ((), (), s32[]{:S(2)}) async-start(), calls=%async_computation.3 | async-start | bytes 8519680 | tf_op jit(solution)/shard_map/all_gather | solution.py:82
  7.9 264.6 %reduce-scatter.4.cloned.1.call-start = ((), (), s32[]{:S(2)}) async-start(), calls=%async_computation.4 | async-start | bytes 25165824 | tf_op jit(solution)/shard_map/reduce_scatter | solution.py:107
  102.5 52.8 %copy-start.8 = (bf16[256,1024]{1,0:T(8,128)(2,1)S(1)}, bf16[256,1024]{1,0:T(8,128)(2,1)}, u32[]{:S(2)}) copy-start(bf16[256,1024]{1,0:T(8,128)(2,1)} %param.6) | copy-start | bytes 1572868
  105.4 26.2 %collective-permute-start.4 = (f32[256,1024]{1,0:T(8,128)}, f32[256,1024]{1,0:T(8,128)S(1)}, u32[]{:S(2)}, u32[]{:S(2)}) collective-permute-start(f32[256,1024]{1,0:T(8,128)} %get-tuple-element.20), channel_id=1, source_target_pairs={{0,1},{1,2},{2,3},{3,0},{4,5},{5,6},{6,7},{7,4},{8,9},{9,10},{10,1... | collective-permute-start | bytes 3145736 | tf_op jit(solution)/shard_map/ppermute | solution.py:56
  106.9 25.7 %collective-permute-start.6 = (f32[256,1024]{1,0:T(8,128)}, f32[256,1024]{1,0:T(8,128)}, u32[]{:S(2)}, u32[]{:S(2)}) collective-permute-start(f32[256,1024]{1,0:T(8,128)} %get-tuple-element.21), channel_id=1, source_target_pairs={{0,3},{1,0},{2,1},{3,2},{4,7},{5,4},{6,5},{7,6},{8,11},{9,8},{10,9... | collective-permute-start | bytes 3145736 | tf_op jit(solution)/shard_map/ppermute | solution.py:56
  107.5 47.9 %collective-permute-start.5 = (f32[256,1024]{1,0:T(8,128)}, f32[256,1024]{1,0:T(8,128)}, u32[]{:S(2)}, u32[]{:S(2)}) collective-permute-start(f32[256,1024]{1,0:T(8,128)} %get-tuple-element.22), channel_id=1, source_target_pairs={{0,2},{1,3},{2,0},{3,1},{4,6},{5,7},{6,4},{7,5},{8,10},{9,11},{10,... | collective-permute-start | bytes 3145736 | tf_op jit(solution)/shard_map/ppermute | solution.py:56
  159.1 3.9 collective-permute-start.7
  176.4 9.3 %collective-permute-start = (bf16[127,1024]{1,0:T(8,128)(2,1)S(1)}, bf16[127,1024]{1,0:T(8,128)(2,1)S(1)}, u32[]{:S(2)}, u32[]{:S(2)}) collective-permute-start(bf16[127,1024]{1,0:T(8,128)(2,1)S(1)} %slice.26), channel_id=1, source_target_pairs={{0,4},{4,8},{8,12},{12,16},{16,20},{20,24},{24,28},{28,32},{32,36}... | collective-permute-start | bytes 780296 | tf_op jit(solution)/shard_map/ppermute | solution.py:25
  197.8 14.2 %collective-permute-start.3 = (bf16[256,1024]{1,0:T(8,128)(2,1)S(1)}, bf16[256,1024]{1,0:T(8,128)(2,1)S(1)}, u32[]{:S(2)}, u32[]{:S(2)}) collective-permute-start(bf16[256,1024]{1,0:T(8,128)(2,1)S(1)} %get-tuple-element.35), channel_id=1, source_target_pairs={{0,3},{1,0},{2,1},{3,2},{4,7},{5,4},{6,5},{7,6},{8,11},{9,8},{10,9... | collective-permute-start | bytes 1572872 | tf_op jit(solution)/shard_map/ppermute | solution.py:44
  198.7 23.6 %collective-permute-start.2 = (bf16[256,1024]{1,0:T(8,128)(2,1)S(1)}, bf16[256,1024]{1,0:T(8,128)(2,1)S(1)}, u32[]{:S(2)}, u32[]{:S(2)}) collective-permute-start(bf16[256,1024]{1,0:T(8,128)(2,1)S(1)} %get-tuple-element.35), channel_id=1, source_target_pairs={{0,2},{1,3},{2,0},{3,1},{4,6},{5,7},{6,4},{7,5},{8,10},{9,11},{10,... | collective-permute-start | bytes 1572872 | tf_op jit(solution)/shard_map/ppermute | solution.py:44
  199.6 25.5 %collective-permute-start.1 = (bf16[256,1024]{1,0:T(8,128)(2,1)S(1)}, bf16[256,1024]{1,0:T(8,128)(2,1)S(1)}, u32[]{:S(2)}, u32[]{:S(2)}) collective-permute-start(bf16[256,1024]{1,0:T(8,128)(2,1)S(1)} %get-tuple-element.35), channel_id=1, source_target_pairs={{0,1},{1,2},{2,3},{3,0},{4,5},{5,6},{6,7},{7,4},{8,9},{9,10},{10,1... | collective-permute-start | bytes 1572872 | tf_op jit(solution)/shard_map/ppermute | solution.py:44
  242.6 138.2 %reduce-scatter.6.cloned.1.call-start = ((), (), s32[]{:S(2)}) async-start(), calls=%async_computation.5 | async-start | bytes 9437184 | tf_op jit(solution)/shard_map/reduce_scatter | solution.py:107
  272.5 171.2 %reduce-scatter.8.cloned.1.call-start = ((), (), s32[]{:S(2)}) async-start(), calls=%async_computation.6 | async-start | bytes 1310720 | tf_op jit(solution)/shard_map/reduce_scatter | solution.py:107
  284.9 14.1 %collective-permute-start.8 = (f32[1024,128]{0,1:T(8,128)S(1)}, f32[1024,128]{0,1:T(8,128)S(1)}, u32[]{:S(2)}, u32[]{:S(2)}) collective-permute-start(f32[1024,128]{0,1:T(8,128)S(1)} %bitcast.52), channel_id=1, source_target_pairs={{0,64},{64,0},{128,192},{192,128},{1,65},{65,1},{129,193},{193,129... | collective-permute-start | bytes 1572872 | tf_op jit(solution)/shard_map/ppermute | solution.py:64
  299.1 14.8 %collective-permute-start.9 = (f32[1024,128]{0,1:T(8,128)S(1)}, f32[1024,128]{0,1:T(8,128)S(1)}, u32[]{:S(2)}, u32[]{:S(2)}) collective-permute-start(f32[1024,128]{0,1:T(8,128)S(1)} %bitcast_add_fusion), channel_id=1, source_target_pairs={{0,128},{64,192},{128,0},{192,64},{1,129},{65,193},{129,1},{193,65... | collective-permute-start | bytes 1572872 | tf_op jit(solution)/shard_map/ppermute | solution.py:64
  314.0 66.9 %collective-permute-start.10 = (f32[1024,128]{0,1:T(8,128)S(1)}, f32[1024,128]{0,1:T(8,128)S(1)}, u32[]{:S(2)}, u32[]{:S(2)}) collective-permute-start(f32[1024,128]{0,1:T(8,128)S(1)} %add.103), channel_id=1, source_target_pairs={{0,8},{8,0},{16,24},{24,16},{32,40},{40,32},{48,56},{56,48},{1,9},... | collective-permute-start | bytes 1572872 | tf_op jit(solution)/shard_map/ppermute | solution.py:64
  380.8 55.2 %copy-start.15 = (bf16[256,1024]{1,0:T(8,128)(2,1)S(1)}, bf16[256,1024]{1,0:T(8,128)(2,1)}, u32[]{:S(2)}) copy-start(bf16[256,1024]{1,0:T(8,128)(2,1)} %get-tuple-element.24) | copy-start | bytes 1572868
  380.8 55.2 %copy-start.16 = (bf16[256,1024]{1,0:T(8,128)(2,1)S(1)}, bf16[256,1024]{1,0:T(8,128)(2,1)}, u32[]{:S(2)}) copy-start(bf16[256,1024]{1,0:T(8,128)(2,1)} %get-tuple-element.25) | copy-start | bytes 1572868
  380.8 55.2 %copy-start.17 = (bf16[256,1024]{1,0:T(8,128)(2,1)S(1)}, bf16[256,1024]{1,0:T(8,128)(2,1)}, u32[]{:S(2)}) copy-start(bf16[256,1024]{1,0:T(8,128)(2,1)} %get-tuple-element.26) | copy-start | bytes 1572868
  380.9 55.2 %copy-start.18 = (bf16[256,1024]{1,0:T(8,128)(2,1)S(1)}, bf16[256,1024]{1,0:T(8,128)(2,1)}, u32[]{:S(2)}) copy-start(bf16[256,1024]{1,0:T(8,128)(2,1)} %get-tuple-element.27) | copy-start | bytes 1572868
  380.9 25.8 %collective-permute-start.11 = (f32[1024,128]{0,1:T(8,128)S(1)}, f32[1024,128]{0,1:T(8,128)S(1)}, u32[]{:S(2)}, u32[]{:S(2)}) collective-permute-start(f32[1024,128]{0,1:T(8,128)S(1)} %add.104), channel_id=1, source_target_pairs={{0,16},{8,24},{16,0},{24,8},{32,48},{40,56},{48,32},{56,40},{1,17}... | collective-permute-start | bytes 1572872 | tf_op jit(solution)/shard_map/ppermute | solution.py:64
  406.8 29.1 %collective-permute-start.12 = (f32[1024,128]{0,1:T(8,128)S(1)}, f32[1024,128]{0,1:T(8,128)S(1)}, u32[]{:S(2)}, u32[]{:S(2)}) collective-permute-start(f32[1024,128]{0,1:T(8,128)S(1)} %add.105), channel_id=1, source_target_pairs={{0,32},{8,40},{16,48},{24,56},{32,0},{40,8},{48,16},{56,24},{1,33}... | collective-permute-start | bytes 1572872 | tf_op jit(solution)/shard_map/ppermute | solution.py:64
  435.9 6.7 %collective-permute-start.13 = (f32[1024,128]{0,1:T(8,128)S(1)}, f32[1024,128]{0,1:T(8,128)S(1)}, u32[]{:S(2)}, u32[]{:S(2)}) collective-permute-start(f32[1024,128]{0,1:T(8,128)S(1)} %add.106), channel_id=1, source_target_pairs={{0,4},{4,0},{1,5},{5,1},{2,6},{6,2},{3,7},{7,3},{8,12},{12,8},{9,1... | collective-permute-start | bytes 1572872 | tf_op jit(solution)/shard_map/ppermute | solution.py:64
  (13 other events, 128.1 us)
Sparse Core Ops, SparseCore 0:
  10.8 85.9 all-gather.1
  242.7 29.6 reduce-scatter.3
  275.0 105.6 reduce-scatter.5
  383.8 26.7 reduce-scatter.7
